TPU v7x, 256 devices: a whole 4x4x8 slice. The times are simulated.
256 devices in a mesh: grp: 4 (over y_lo, core), shard: 64 (over z, x, y_hi).
Axes of the slice: x: 4, y: 4 (y_hi: 2, y_lo: 2; y = y_hi * 2 + y_lo), z: 8, core: 2. Of those that a mesh axis runs over, the one named last changes fastest.
Arguments:
- layer_inner: float32 [4, 1600, 1600], P('grp', 'shard'), may hold values from -6 to 6
- layer_weights: float32 [1600, 1600], P('shard'), may hold values from -6 to 6
- layer_moment: float32 [1600, 1600], P('shard'), may hold values from -6 to 6
- embed_inner: float32 [4, 25600, 1600], P('grp', 'shard'), may hold values from -6 to 6
- embed_weights: float32 [25600, 1600], P(('shard', 'grp')), may hold values from -6 to 6
- embed_moment: float32 [25600, 1600], P(('shard', 'grp')), may hold values from -6 to 6
- basis: float32 [1600, 64], replicated, may hold values from -0.15625 to 0.15625
Outputs:
- layer_new: float32 [1600, 1600], P('shard')
- layer_moment_new: float32 [1600, 1600], P('shard')
- layer_copy: bfloat16 [1600, 1600], replicated
- embed_new: float32 [25600, 1600], P(('shard', 'grp'))
- embed_moment_new: float32 [25600, 1600], P(('shard', 'grp'))
All inputs are finite; a program needn't handle non-finite values.
Results may differ from a plain program's by a relative error of at most 0.0015.
Values may be sent and summed in bfloat16 or wider, within the bound.
No kernel may reach another device: no remote copies, remote signals or barrier semaphores. Data moves between devices by JAX's collectives and lax.ppermute only.
A program may use at most 128 MiB of HBM per device.

v0:
```python
import jax
import jax.numpy as jnp
from jax import lax
from jax.sharding import PartitionSpec as P

outer_rate = 0.7
momentum_coef = 0.9


def nesterov(weights, moment, average):
    moment_new = momentum_coef * moment + average
    return (weights - outer_rate * (average + momentum_coef * moment_new), moment_new)


def per_device(
    layer_inner, layer_weights, layer_moment, embed_inner, embed_weights, embed_moment, basis
):
    groups = lax.axis_size("grp")
    inner_proj = jnp.dot(embed_inner[0], basis, precision=lax.Precision.HIGHEST)
    mean_proj = (
        lax.psum_scatter(
            inner_proj.astype(jnp.bfloat16), "grp", scatter_dimension=0, tiled=True
        ).astype(jnp.float32)
        / groups
    )
    factors = jnp.dot(embed_weights, basis, precision=lax.Precision.HIGHEST) - mean_proj
    embed_step = jnp.dot(factors, basis.T, precision=lax.Precision.HIGHEST)
    embed_new, embed_moment_new = nesterov(embed_weights, embed_moment, embed_step)
    own_diff = layer_weights - layer_inner[0]
    average = lax.psum(own_diff, "grp") / groups
    layer_new, layer_moment_new = nesterov(layer_weights, layer_moment, average)
    layer_copy = lax.all_gather(layer_new.astype(jnp.bfloat16), "shard", axis=0, tiled=True)
    return (layer_new, layer_moment_new, layer_copy, embed_new, embed_moment_new)


def solution(mesh):
    in_specs = (
        P("grp", "shard", None),
        P("shard", None),
        P("shard", None),
        P("grp", "shard", None),
        P(("shard", "grp"), None),
        P(("shard", "grp"), None),
        P(),
    )
    out_specs = (
        P("shard", None),
        P("shard", None),
        P(),
        P(("shard", "grp"), None),
        P(("shard", "grp"), None),
    )
    return jax.shard_map(
        per_device, mesh=mesh, in_specs=in_specs, out_specs=out_specs, check_vma=False
    )
```

profile of v0, /device:TPU:2, one launch (start us, length us, event | category | flops | bytes accessed | tf_op | source)
XLA Modules:
  0.0 215.2 jit_solution(13905958962458578667)
XLA Ops:
  7.2 0.0 copy-start
  7.2 0.0 copy-start.1
  7.2 0.0 all-reduce.4.cloned.1.call-start
  7.2 1.9 bitcast_subtract_fusion
  9.1 0.0 all-reduce.4.cloned.1.call-update
  9.1 0.0 all-gather.3.cloned.1.call-start
  9.2 46.2 %all-reduce.4.cloned.1.call-done = f32[25,1600]{1,0:T(8,128)} async-done(((f32[25,1600]{1,0:T(8,128)}), f32[25,1600]{1,0:T(8,128)}) %all-reduce.4.cloned.1.call-update) | async-done | bytes 160016 | tf_op jit(solution)/shard_map/psum | solution.py:30
  55.4 2.0 convert_bitcast_fusion
  57.4 0.0 copy-start.2
  57.4 0.0 all-gather.3.cloned.1.call-update
  57.4 0.0 copy-done
  57.4 3.6 %fusion.3 = bf16[400,64]{0,1:T(8,128)(2,1)S(1)} fusion(f32[1600,64]{0,1:T(8,128)} %param.13, f32[1,400,1600]{2,1,0:T(8,128)S(1)} %copy-done), kind=kOutput, calls=%fused_computation.2 | convolution fusion | flops 491545600 | bytes 3020800 | tf_op jit(solution)/shard_map/dot_general | solution.py:19
  61.0 0.1 copy.12
  61.2 8.3 %fusion = bf16[112,64]{1,0:T(8,128)(2,1)S(1)} fusion(bf16[400,64]{1,0:T(8,128)(2,1)S(1)} %copy.12), kind=kCustom, calls=%all-reduce-scatter | all-reduce-scatter fusion | flops 28673 | bytes 66560
  69.5 1.3 collective-permute-start
  70.8 0.0 copy-done.1
  70.8 2.0 fusion.12
  72.7 0.0 copy-done.2
  72.7 0.6 dynamic-slice.4
  74.0 0.0 collective-permute-done
  74.0 0.3 concatenate
  74.3 0.1 copy.13
  74.4 3.3 %multiply_subtract_fusion = (f32[100,1600]{1,0:T(8,128)}, f32[100,1600]{1,0:T(8,128)}) fusion(f32[100,1600]{1,0:T(8,128)} %param.11, f32[100,1600]{1,0:T(8,128)} %param.12, f32[1600,64]{0,1:T(8,128)S(1)} %copy-done.1, f32[100,64]{0,1:T(8,128)S(1)} %fusion.12, bf16[100,64]{0,1:T(8,128)(2,1)S(1)} %copy.13), kind=kOutput, calls=%fused_computation.3 | convolution fusion | flops 123859200 | bytes 3008000 | tf_op jit(solution)/shard_map/dot_general | solution.py:27
  77.6 122.1 %all-gather.3.cloned.1.call-done = bf16[64,25,1600]{2,1,0:T(8,128)(2,1)} async-done(((bf16[1,25,1600]{2,1,0:T(8,128)(2,1)}), bf16[64,25,1600]{2,1,0:T(8,128)(2,1)}) %all-gather.3.cloned.1.call-update) | async-done | bytes 5120016 | tf_op jit(solution)/shard_map/all_gather | solution.py:32
  199.7 8.6 %reshape.11 = bf16[1600,1600]{1,0:T(8,128)(2,1)} reshape(bf16[64,25,1600]{2,1,0:T(8,128)(2,1)} %all-gather.3.cloned.1.call-done) | data formatting | bytes 10240000
  (2 shorter events, 0.0 us)
Async XLA Ops:
  7.2 50.2 %copy-start = (f32[1,400,1600]{2,1,0:T(8,128)S(1)}, f32[1,400,1600]{2,1,0:T(8,128)}, u32[]{:S(2)}) copy-start(f32[1,400,1600]{2,1,0:T(8,128)} %param.10) | copy-start | bytes 7680004
  7.2 63.6 %copy-start.1 = (f32[1600,64]{0,1:T(8,128)S(1)}, f32[1600,64]{0,1:T(8,128)}, u32[]{:S(2)}) copy-start(f32[1600,64]{0,1:T(8,128)} %param.13) | copy-start | bytes 1228804
  7.2 48.2 %all-reduce.4.cloned.1.call-start = ((), (), s32[]{:S(2)}) async-start(), calls=%async_computation | async-start | bytes 425984 | tf_op jit(solution)/shard_map/psum | solution.py:30
  9.1 190.6 %all-gather.3.cloned.1.call-start = ((), (), s32[]{:S(2)}) async-start(), calls=%async_computation.1 | async-start | bytes 6922240 | tf_op jit(solution)/shard_map/all_gather | solution.py:32
  57.4 15.4 %copy-start.2 = (u32[256]{0:T(256)S(1)}, u32[256]{0:T(256)}, u32[]{:S(2)}) copy-start(u32[256]{0:T(256)} %constant.19) | copy-start | bytes 3076
  69.5 4.5 %collective-permute-start = (bf16[36,64]{1,0:T(8,128)(2,1)S(1)}, bf16[36,64]{1,0:T(8,128)(2,1)S(1)}, u32[]{:S(2)}, u32[]{:S(2)}) collective-permute-start(bf16[36,64]{1,0:T(8,128)(2,1)S(1)} %slice), channel_id=1, source_target_pairs={{0,64},{64,128},{128,192},{1,65},{65,129},{129,193},{2,66},{66,130... | collective-permute-start | bytes 13832
Sparse Core Ops, SparseCore 0:
  11.2 44.1 all-reduce.3
  59.6 140.0 all-gather.2
where the time goes:
time: 216 us; the launch traced here: 215 us
  waiting for transfers between devices  168 us (78%)
  between operations  14.8 us (7%)
  local copies, waits for them, and re-layouts  9.74 us (5%)
  matrix products  8.84 us (4%)
  blocking collectives  8.27 us (4%)
  other arithmetic  3.85 us (2%)
    all_gather x1, waiting for transfers between devices, per_device(): lax.all_gather(layer_new.astype(jnp.bfloat16), 'shard', axis=0, tiled=True)  122 us
    psum x1, waiting for transfers between devices, per_device(): average = lax.psum(own_diff, 'grp') / groups  46.2 us
    unnamed x11, local copies, waits for them, and re-layouts  9.52 us
    unnamed x1, blocking collectives  8.27 us
  transfers between devices with their start and end apart: 3, of which 2 were waited for; matrix products, arithmetic and copies ran while one was open for 8% of the time, Pallas kernels for 0%

commit v1 on v0

--- a/solution.py
+++ b/solution.py
@@ -27,7 +27,7 @@
     embed_step = jnp.dot(factors, basis.T, precision=lax.Precision.HIGHEST)
     embed_new, embed_moment_new = nesterov(embed_weights, embed_moment, embed_step)
     own_diff = layer_weights - layer_inner[0]
-    average = lax.psum(own_diff, "grp") / groups
+    average = jnp.sum(lax.all_gather(own_diff, "grp"), axis=0) / groups
     layer_new, layer_moment_new = nesterov(layer_weights, layer_moment, average)
     layer_copy = lax.all_gather(layer_new.astype(jnp.bfloat16), "shard", axis=0, tiled=True)
     return (layer_new, layer_moment_new, layer_copy, embed_new, embed_moment_new)

time: 216 us -> 179 us (0.83)
  waiting for transfers between devices: 168 us -> 123 us
  blocking collectives: 8.27 us -> 17.8 us
    psum x1 -> x0, waiting for transfers between devices: 46.2 us -> none  [per_device(): average = lax.psum(own_diff, 'grp') / groups]
    all_gather x0 -> x1, blocking collectives: none -> 9.49 us  [per_device(): average = jnp.sum(lax.all_gather(own_diff, 'grp'), axis=0) / groups]
    unnamed x11 -> x13, local copies, waits for them, and re-layouts: 9.52 us -> 9.52 us
  transfers between devices with their start and end apart: 3 -> 2, of which waited for: 2 -> 1; matrix products, arithmetic and copies ran while one was open for 8% -> 10% of each run, Pallas kernels for 0% -> 0%
where the time goes in v1:
time: 179 us; the launch traced here: 178 us
  waiting for transfers between devices  123 us (69%)
  blocking collectives  17.8 us (10%)
  between operations  14.8 us (8%)
  local copies, waits for them, and re-layouts  9.74 us (5%)
  matrix products  7.87 us (4%)
  other arithmetic  4.25 us (2%)
    all_gather x1, waiting for transfers between devices, per_device(): lax.all_gather(layer_new.astype(jnp.bfloat16), 'shard', axis=0, tiled=True)  123 us
    unnamed x13, local copies, waits for them, and re-layouts  9.52 us
    all_gather x1, blocking collectives, per_device(): average = jnp.sum(lax.all_gather(own_diff, 'grp'), axis=0) / groups  9.49 us
    unnamed x1, blocking collectives  8.27 us
  transfers between devices with their start and end apart: 2, of which 1 were waited for; matrix products, arithmetic and copies ran while one was open for 10% of the time, Pallas kernels for 0%

profile of v1, /device:TPU:2, one launch (start us, length us, event | category | flops | bytes accessed | tf_op | source)
XLA Modules:
  0.0 178.3 jit_solution(7045176719534472360)
XLA Ops:
  7.2 0.0 copy-start
  7.2 0.0 copy-start.2
  7.2 0.0 copy-start.1
  7.2 0.0 all-gather.5.cloned.1.call-start
  7.2 1.2 fusion.6
  8.5 9.5 %all-gather.1 = f32[4,25,1600]{2,1,0:T(8,128)} all-gather(f32[1,25,1600]{2,1,0:T(8,128)S(1)} %fusion.6), channel_id=2, replica_groups=mesh['grp'=4,'shard'=64] {'grp'}, dimensions={0}, use_global_device_ids=true | all-gather | bytes 800000 | tf_op jit(solution)/shard_map/all_gather | solution.py:30
  18.0 1.2 reduce_sum.9
  19.2 0.0 copy-done.2
  19.2 1.8 %convert_bitcast_fusion = (bf16[1,25,1600]{2,1,0:T(8,128)(2,1)}, f32[25,1600]{1,0:T(8,128)}, f32[25,1600]{1,0:T(8,128)}) fusion(f32[25,1600]{1,0:T(8,128)S(1)} %copy-done.2, f32[25,1600]{1,0:T(8,128)S(1)} %reduce_sum.9, f32[25,1600]{1,0:T(8,128)} %param.9), kind=kLoop, calls=%fused_computation.9 | loop fusion | flops 320000 | bytes 880000
  21.0 0.0 copy-start.3
  21.0 0.0 all-gather.5.cloned.1.call-update
  21.0 0.0 copy-done
  21.0 0.0 copy-done.1
  21.0 2.6 %fusion.3 = bf16[400,64]{0,1:T(8,128)(2,1)S(1)} fusion(f32[1600,64]{0,1:T(8,128)S(1)} %copy-done.1, f32[1,400,1600]{2,1,0:T(8,128)S(1)} %copy-done), kind=kOutput, calls=%fused_computation.2 | convolution fusion | flops 491545600 | bytes 3020800 | tf_op jit(solution)/shard_map/dot_general | solution.py:19
  23.7 0.1 copy.12
  23.8 8.3 %fusion = bf16[112,64]{1,0:T(8,128)(2,1)S(1)} fusion(bf16[400,64]{1,0:T(8,128)(2,1)S(1)} %copy.12), kind=kCustom, calls=%all-reduce-scatter | all-reduce-scatter fusion | flops 28673 | bytes 66560
  32.1 1.3 collective-permute-start
  33.4 2.0 %fusion.13 = f32[100,64]{0,1:T(8,128)S(1)} fusion(f32[100,1600]{1,0:T(8,128)} %param.11, f32[1600,64]{0,1:T(8,128)S(1)} %copy-done.1), kind=kOutput, calls=%fused_computation.17 | convolution fusion | flops 122880000 | bytes 1075200 | tf_op jit(solution)/shard_map/dot_general | solution.py:26
  35.4 0.0 copy-done.3
  35.4 0.6 dynamic-slice.4
  36.6 0.0 collective-permute-done
  36.6 0.3 concatenate
  36.9 0.1 copy.13
  37.0 3.3 %multiply_subtract_fusion = (f32[100,1600]{1,0:T(8,128)}, f32[100,1600]{1,0:T(8,128)}) fusion(f32[100,1600]{1,0:T(8,128)} %param.11, f32[100,1600]{1,0:T(8,128)} %param.12, f32[1600,64]{0,1:T(8,128)S(1)} %copy-done.1, f32[100,64]{0,1:T(8,128)S(1)} %fusion.13, bf16[100,64]{0,1:T(8,128)(2,1)S(1)} %copy.13), kind=kOutput, calls=%fused_computation.3 | convolution fusion | flops 123859200 | bytes 3008000 | tf_op jit(solution)/shard_map/dot_general | solution.py:27
  40.3 122.5 %all-gather.5.cloned.1.call-done = bf16[64,25,1600]{2,1,0:T(8,128)(2,1)} async-done(((bf16[1,25,1600]{2,1,0:T(8,128)(2,1)}), bf16[64,25,1600]{2,1,0:T(8,128)(2,1)}) %all-gather.5.cloned.1.call-update) | async-done | bytes 5120016 | tf_op jit(solution)/shard_map/all_gather | solution.py:32
  162.8 8.6 %reshape.14 = bf16[1600,1600]{1,0:T(8,128)(2,1)} reshape(bf16[64,25,1600]{2,1,0:T(8,128)(2,1)} %all-gather.5.cloned.1.call-done) | data formatting | bytes 10240000
  (2 shorter events, 0.0 us)
Async XLA Ops:
  7.2 13.9 %copy-start = (f32[1,400,1600]{2,1,0:T(8,128)S(1)}, f32[1,400,1600]{2,1,0:T(8,128)}, u32[]{:S(2)}) copy-start(f32[1,400,1600]{2,1,0:T(8,128)} %param.10) | copy-start | bytes 7680004
  7.2 12.0 %copy-start.2 = (f32[25,1600]{1,0:T(8,128)S(1)}, f32[25,1600]{1,0:T(8,128)}, u32[]{:S(2)}) copy-start(f32[25,1600]{1,0:T(8,128)} %param.8) | copy-start | bytes 480004
  7.2 13.8 %copy-start.1 = (f32[1600,64]{0,1:T(8,128)S(1)}, f32[1600,64]{0,1:T(8,128)}, u32[]{:S(2)}) copy-start(f32[1600,64]{0,1:T(8,128)} %param.13) | copy-start | bytes 1228804
  7.2 155.6 %all-gather.5.cloned.1.call-start = ((), (), s32[]{:S(2)}) async-start(), calls=%async_computation | async-start | bytes 6922240 | tf_op jit(solution)/shard_map/all_gather | solution.py:32
  21.0 14.4 %copy-start.3 = (u32[256]{0:T(256)S(1)}, u32[256]{0:T(256)}, u32[]{:S(2)}) copy-start(u32[256]{0:T(256)} %constant.21) | copy-start | bytes 3076
  32.1 4.5 %collective-permute-start = (bf16[36,64]{1,0:T(8,128)(2,1)S(1)}, bf16[36,64]{1,0:T(8,128)(2,1)S(1)}, u32[]{:S(2)}, u32[]{:S(2)}) collective-permute-start(bf16[36,64]{1,0:T(8,128)(2,1)S(1)} %slice), channel_id=1, source_target_pairs={{0,64},{64,128},{128,192},{1,65},{65,129},{129,193},{2,66},{66,130... | collective-permute-start | bytes 13832
Sparse Core Ops, SparseCore 0:
  21.1 141.6 all-gather.4

commit v2 on v0

--- a/solution.py
+++ b/solution.py
@@ -29,7 +29,12 @@
     own_diff = layer_weights - layer_inner[0]
     average = lax.psum(own_diff, "grp") / groups
     layer_new, layer_moment_new = nesterov(layer_weights, layer_moment, average)
-    layer_copy = lax.all_gather(layer_new.astype(jnp.bfloat16), "shard", axis=0, tiled=True)
+    layer_copy = jnp.concatenate(
+        lax.all_to_all(
+            jnp.stack([layer_new.astype(jnp.bfloat16)] * lax.axis_size("shard")), "shard", 0, 0
+        ),
+        axis=0,
+    )
     return (layer_new, layer_moment_new, layer_copy, embed_new, embed_moment_new)
 
 

time: 216 us -> 248 us (1.15)
  the two profiles are of different devices: /device:TPU:2 before, /device:TPU:9 now
where the time goes in v2:
time: 248 us; the launch traced here: 247 us
  waiting for transfers between devices  177 us (71%)
  blocking collectives  18 us (7%)
  between operations  14.8 us (6%)
  starting transfers between devices  13.3 us (5%)
  local copies, waits for them, and re-layouts  13.1 us (5%)
  matrix products  7.84 us (3%)
  other arithmetic  3.82 us (2%)
    all_to_all x1, waiting for transfers between devices, per_device(): lax.all_to_all(jnp.stack([layer_new.astype(jnp.bfloat16)] * lax.axis_size...  130 us
    psum x1, waiting for transfers between devices, per_device(): average = lax.psum(own_diff, 'grp') / groups  46.1 us
    unnamed x1, blocking collectives  18 us
    all_to_all x1, starting transfers between devices, per_device(): lax.all_to_all(jnp.stack([layer_new.astype(jnp.bfloat16)] * lax.axis_size...  12 us
    reshape x1, local copies, waits for them, and re-layouts, per_device(): jnp.concatenate(lax.all_to_all(jnp.stack([layer_new.astype(jnp.bfloat16)]...  8.62 us
  transfers between devices with their start and end apart: 3, of which 2 were waited for; matrix products, arithmetic and copies ran while one was open for 11% of the time, Pallas kernels for 0%

profile of v2, /device:TPU:9, one launch (start us, length us, event | category | flops | bytes accessed | tf_op | source)
XLA Modules:
  0.0 247.4 jit_solution(5900573409434700661)
XLA Ops:
  7.2 0.0 copy-start
  7.2 0.0 all-reduce.4.cloned.1.call-start
  7.2 1.9 bitcast_subtract_fusion
  9.1 0.0 all-reduce.4.cloned.1.call-update
  9.1 46.1 %all-reduce.4.cloned.1.call-done = f32[25,1600]{1,0:T(8,128)} async-done(((f32[25,1600]{1,0:T(8,128)}), f32[25,1600]{1,0:T(8,128)}) %all-reduce.4.cloned.1.call-update) | async-done | bytes 160016 | tf_op jit(solution)/shard_map/psum | solution.py:30
  55.3 1.9 fusion.12
  57.2 3.3 %stack.2 = bf16[64,25,1600]{2,1,0:T(8,128)(2,1)} broadcast(bf16[25,1600]{1,0:T(8,128)(2,1)S(1)} %get-tuple-element.7), dimensions={1,2} | broadcast | bytes 5200000 | tf_op jit(solution)/shard_map/stack | solution.py:34
  60.5 0.0 copy-start.1
  60.5 12.0 %all-to-all-start = ((bf16[64,25,1600]{2,1,0:T(8,128)(2,1)}), bf16[64,25,1600]{2,1,0:T(8,128)(2,1)}, u32[]{:S(2)}, u32[]{:S(2)}) async-start(bf16[64,25,1600]{2,1,0:T(8,128)(2,1)} %stack.2), calls=%async_computation | async-start | bytes 13631488 | tf_op jit(solution)/shard_map/all_to_all | solution.py:33
  72.6 0.0 copy-done
  72.6 0.0 copy-done.1
  72.6 0.0 copy-start.2
  72.6 2.6 %fusion.3 = bf16[400,64]{0,1:T(8,128)(2,1)S(1)} fusion(f32[1600,64]{0,1:T(8,128)S(1)} %copy-done.1, f32[1,400,1600]{2,1,0:T(8,128)S(1)} %copy-done), kind=kOutput, calls=%fused_computation.2 | convolution fusion | flops 491545600 | bytes 3020800 | tf_op jit(solution)/shard_map/dot_general | solution.py:19
  75.2 0.1 copy.12
  75.3 18.0 %fusion = bf16[112,64]{1,0:T(8,128)(2,1)S(1)} fusion(bf16[400,64]{1,0:T(8,128)(2,1)S(1)} %copy.12), kind=kCustom, calls=%all-reduce-scatter | all-reduce-scatter fusion | flops 28673 | bytes 66560
  93.4 1.3 collective-permute-start
  94.7 2.0 fusion.13
  96.7 0.0 copy-done.2
  96.7 0.6 dynamic-slice.4
  97.9 0.0 collective-permute-done
  97.9 0.3 concatenate
  98.2 0.1 copy.13
  98.3 3.2 %multiply_subtract_fusion = (f32[100,1600]{1,0:T(8,128)}, f32[100,1600]{1,0:T(8,128)}) fusion(f32[100,1600]{1,0:T(8,128)} %param.11, f32[100,1600]{1,0:T(8,128)} %param.12, f32[1600,64]{0,1:T(8,128)S(1)} %copy-done.1, f32[100,64]{0,1:T(8,128)S(1)} %fusion.13, bf16[100,64]{0,1:T(8,128)(2,1)S(1)} %copy.13), kind=kOutput, calls=%fused_computation.3 | convolution fusion | flops 123859200 | bytes 3008000 | tf_op jit(solution)/shard_map/dot_general | solution.py:27
  101.6 130.4 %all-to-all-done = bf16[64,25,1600]{2,1,0:T(8,128)(2,1)} async-done(((bf16[64,25,1600]{2,1,0:T(8,128)(2,1)}), bf16[64,25,1600]{2,1,0:T(8,128)(2,1)}, u32[]{:S(2)}, u32[]{:S(2)}) %all-to-all-start) | async-done | bytes 5120032 | tf_op jit(solution)/shard_map/all_to_all | solution.py:33
  232.0 8.6 %reshape.15 = bf16[1600,1600]{1,0:T(8,128)(2,1)} reshape(bf16[64,25,1600]{2,1,0:T(8,128)(2,1)} %all-to-all-done) | data formatting | bytes 10240000 | tf_op jit(solution)/shard_map/reshape | solution.py:32
  (2 shorter events, 0.0 us)
Async XLA Ops:
  7.2 65.4 %copy-start = (f32[1,400,1600]{2,1,0:T(8,128)S(1)}, f32[1,400,1600]{2,1,0:T(8,128)}, u32[]{:S(2)}) copy-start(f32[1,400,1600]{2,1,0:T(8,128)} %param.10) | copy-start | bytes 7680004
  7.2 48.1 %all-reduce.4.cloned.1.call-start = ((), (), s32[]{:S(2)}) async-start(), calls=%async_computation.1 | async-start | bytes 425984 | tf_op jit(solution)/shard_map/psum | solution.py:30
  60.5 12.0 %copy-start.1 = (f32[1600,64]{0,1:T(8,128)S(1)}, f32[1600,64]{0,1:T(8,128)}, u32[]{:S(2)}) copy-start(f32[1600,64]{0,1:T(8,128)} %param.13) | copy-start | bytes 1228804
  60.5 171.4 %all-to-all-start = ((bf16[64,25,1600]{2,1,0:T(8,128)(2,1)}), bf16[64,25,1600]{2,1,0:T(8,128)(2,1)}, u32[]{:S(2)}, u32[]{:S(2)}) async-start(bf16[64,25,1600]{2,1,0:T(8,128)(2,1)} %stack.2), calls=%async_computation | async-start | bytes 13631488 | tf_op jit(solution)/shard_map/all_to_all | solution.py:33
  72.6 24.1 %copy-start.2 = (u32[256]{0:T(256)S(1)}, u32[256]{0:T(256)}, u32[]{:S(2)}) copy-start(u32[256]{0:T(256)} %constant.19) | copy-start | bytes 3076
  93.4 4.5 %collective-permute-start = (bf16[36,64]{1,0:T(8,128)(2,1)S(1)}, bf16[36,64]{1,0:T(8,128)(2,1)S(1)}, u32[]{:S(2)}, u32[]{:S(2)}) collective-permute-start(bf16[36,64]{1,0:T(8,128)(2,1)S(1)} %slice), channel_id=1, source_target_pairs={{0,64},{64,128},{128,192},{1,65},{65,129},{129,193},{2,66},{66,130... | collective-permute-start | bytes 13832
Sparse Core Ops, SparseCore 0:
  11.2 44.0 all-reduce.3
